TPU v7x, 128 devices: a whole 4x4x4 slice. The times are simulated.
128 devices in a mesh: grp: 8 (over z, core), dev: 16 (over y, x).
Axes of the slice: x: 4, y: 4, z: 4, core: 2. Of those that a mesh axis runs over, the one named last changes fastest.
Arguments:
- positions: float32 [3, 131072], P(None, ('grp', 'dev')), may hold values from -3 to 3
- velocities: float32 [3, 131072], P(None, ('grp', 'dev')), may hold values from -5 to 5
- accelerations: float32 [3, 131072], P(None, ('grp', 'dev')), may hold values from -3 to 3
- jerks: float32 [3, 131072], P(None, ('grp', 'dev')), may hold values from -3 to 3
- levels: int32 [131072], P(('grp', 'dev')), may hold values from 0 to 5
- counts: int32 [2, 128], replicated, may hold values from 1 to 256, 16384 in all within a row
- active_rows: int32 [2, 32768], P(None, ('grp', 'dev')), may hold values from 0 to 1023, as said below
Outputs:
- new_positions: float32 [3, 131072], P(None, ('grp', 'dev'))
- new_velocities: float32 [3, 131072], P(None, ('grp', 'dev'))
- new_accelerations: float32 [3, 131072], P(None, ('grp', 'dev'))
- new_jerks: float32 [3, 131072], P(None, ('grp', 'dev'))
Inputs may be any that keep to these rules, and one draw needn't show every extreme that they name: In each step the 128 counts sum to exactly 16384 and the largest of them is exactly 256. `active_rows`: for each step and device, the 256 entries of the device's slots are distinct indices of that device's own stars; only the first counts of them are live.
All inputs are finite; a program needn't handle non-finite values.
Results may differ from a plain program's by a relative error of at most 0.00022.
Values sent between devices are 32-bit elements; how exact they have to be, the bound alone decides.
No kernel may reach another device: no remote copies, remote signals or barrier semaphores. Data moves between devices by JAX's collectives and lax.ppermute only.
A program may use at most 128 MiB of HBM per device.

v0:
```python
import math
import jax
import jax.numpy as jnp
from jax import lax
from jax.sharding import PartitionSpec as P

tick_length = 1.0 / 128.0


def pair_block(targets, src_pos, src_vel, mass, soft_sq):
    gap_x = src_pos[0][None, :] - targets[0][:, None]
    gap_y = src_pos[1][None, :] - targets[1][:, None]
    gap_z = src_pos[2][None, :] - targets[2][:, None]
    drift_x = src_vel[0][None, :] - targets[3][:, None]
    drift_y = src_vel[1][None, :] - targets[4][:, None]
    drift_z = src_vel[2][None, :] - targets[5][:, None]
    squared = gap_x * gap_x + gap_y * gap_y + gap_z * gap_z + soft_sq
    inverse = lax.rsqrt(squared)
    weight = mass * inverse * inverse * inverse
    along = 3.0 * (gap_x * drift_x + gap_y * drift_y + gap_z * drift_z) * inverse * inverse
    return jnp.stack(
        [
            jnp.sum(weight * gap_x, axis=1),
            jnp.sum(weight * gap_y, axis=1),
            jnp.sum(weight * gap_z, axis=1),
            jnp.sum(weight * (drift_x - along * gap_x), axis=1),
            jnp.sum(weight * (drift_y - along * gap_y), axis=1),
            jnp.sum(weight * (drift_z - along * gap_z), axis=1),
        ]
    )


def block_terms(packed, src_pos, src_vel, mass, soft_sq):
    width, total = packed.shape
    block = math.gcd(total, 2048)
    grouped = packed.reshape(width, total // block, block).transpose(1, 0, 2)
    result = lax.map(lambda targets: pair_block(targets, src_pos, src_vel, mass, soft_sq), grouped)
    return result.transpose(1, 0, 2).reshape(width, total)


def predict(positions, velocities, accelerations, jerks, elapsed):
    span = elapsed[None, :]
    pred_pos = (
        positions
        + span * velocities
        + 0.5 * span * span * accelerations
        + span * span * span / 6.0 * jerks
    )
    pred_vel = velocities + span * accelerations + 0.5 * span * span * jerks
    return (pred_pos, pred_vel)


def correct(old_pos, old_vel, old_acc, old_jerk, force, jerk_new, span):
    span = span[None, :]
    new_vel = old_vel + 0.5 * span * (old_acc + force) + span * span / 12.0 * (old_jerk - jerk_new)
    new_pos = old_pos + 0.5 * span * (old_vel + new_vel) + span * span / 12.0 * (old_acc - force)
    return (new_pos, new_vel)


def shards(positions, velocities, accelerations, jerks, levels, counts, active_rows):
    devices_all = lax.axis_size("grp") * lax.axis_size("dev")
    my_rank = lax.axis_index("grp") * lax.axis_size("dev") + lax.axis_index("dev")
    star_dev = positions.shape[1]
    slot_cap = active_rows.shape[1]
    stars_all = star_dev * devices_all
    live_all = stars_all // 8
    mass = 1.0 / stars_all
    soft_sq = 0.0004 * (131072.0 / stars_all) ** (2.0 / 3.0)
    chunks = 4
    chunk = live_all // chunks
    last_time = -(jnp.left_shift(jnp.int32(1), levels) - 1).astype(jnp.float32) * tick_length
    for step in range(active_rows.shape[0]):
        now = (step + 1) * tick_length
        pred_pos, pred_vel = predict(positions, velocities, accelerations, jerks, now - last_time)
        rows = active_rows[step]
        targets = jnp.concatenate([pred_pos[:, rows], pred_vel[:, rows]], axis=0)
        step_counts = counts[step]
        own_count = step_counts[my_rank]
        inclusive = jnp.cumsum(step_counts).astype(jnp.int32)
        first = inclusive - step_counts
        place = jnp.arange(live_all, dtype=jnp.int32)
        owner = jnp.sum((inclusive[None, :] <= place[:, None]).astype(jnp.int32), axis=1)
        owner = jnp.minimum(owner, devices_all - 1)
        slot = owner * slot_cap + place - first[owner]
        gathered = lax.all_gather(targets[None], ("grp", "dev"), axis=0, tiled=True)
        flat = gathered.transpose(1, 0, 2).reshape(6, devices_all * slot_cap)
        compact = flat[:, slot]
        parts = []
        summed = None
        for c in range(chunks):
            piece = compact[:, c * chunk : (c + 1) * chunk]
            terms = block_terms(piece, pred_pos, pred_vel, mass, soft_sq)
            if summed is not None:
                terms, summed = lax.optimization_barrier((terms, summed))
                parts.append(summed)
            summed = lax.psum(terms, ("grp", "dev"))
        parts.append(summed)
        parts.append(jnp.zeros((6, slot_cap), jnp.float32))
        totals = jnp.concatenate(parts, axis=1)
        own = lax.dynamic_slice_in_dim(totals, first[my_rank], slot_cap, 1)
        span = now - last_time[rows]
        new_pos, new_vel = correct(
            positions[:, rows],
            velocities[:, rows],
            accelerations[:, rows],
            jerks[:, rows],
            own[:3],
            own[3:],
            span,
        )
        live = jnp.arange(slot_cap, dtype=jnp.int32) < own_count
        target = jnp.where(live, rows, star_dev)
        positions = positions.at[:, target].set(new_pos, mode="drop")
        velocities = velocities.at[:, target].set(new_vel, mode="drop")
        accelerations = accelerations.at[:, target].set(own[:3], mode="drop")
        jerks = jerks.at[:, target].set(own[3:], mode="drop")
        last_time = last_time.at[target].set(now, mode="drop")
    return (positions, velocities, accelerations, jerks)


def solution(mesh):
    placed = (
        P(None, ("grp", "dev")),
        P(None, ("grp", "dev")),
        P(None, ("grp", "dev")),
        P(None, ("grp", "dev")),
        P(("grp", "dev")),
        P(),
        P(None, ("grp", "dev")),
    )
    return jax.shard_map(
        shards,
        mesh=mesh,
        in_specs=placed,
        out_specs=(
            P(None, ("grp", "dev")),
            P(None, ("grp", "dev")),
            P(None, ("grp", "dev")),
            P(None, ("grp", "dev")),
        ),
        check_vma=False,
    )
```

profile of v0, /device:TPU:1, one launch (start us, length us, event | category | flops | bytes accessed | tf_op | source)
XLA Modules:
  0.0 1731.8 jit_solution(9103468403013295511)
XLA Ops:
  8.6 2.6 compare_select_fusion.4
  14.8 63.9 %all-gather.2 = f32[128,6,256]{2,1,0:T(8,128)S(1)} all-gather(f32[1,6,256]{2,1,0:T(8,128)S(1)} %maximum_bitcast_fusion), channel_id=2, replica_groups=mesh['grp'=8,'dev'=16] {'grp','dev'}, dimensions={0}, use_global_device_ids=true | all-gather | bytes 792576 | tf_op jit(solution)/shard_map/all_gather | solution.py:85
  78.7 8.4 copy.253
  87.8 2.3 convert_reduce_fusion.1
  90.3 97.2 %gather_fusion.6 = s32[16384]{0:T(1024)S(1)} fusion(s32[128]{0:T(128)S(1)} %get-tuple-element.734, s32[16384]{0:T(1024)S(1)} %broadcast_clamp_fusion.3), kind=kCustom, calls=%fused_computation.6 | custom fusion | bytes 196608 | tf_op jit(solution)/shard_map/gather | solution.py:84
  187.7 60.2 %gather_fusion.7 = f32[16384,6]{1,0:T(8,128)} fusion(f32[6,32768]{0,1:T(8,128)} %bitcast.632, s32[16384]{0:T(1024)S(1)} %broadcast_clamp_fusion.1), kind=kCustom, calls=%fused_computation.7 | custom fusion | bytes 851968 | tf_op jit(solution)/shard_map/gather | solution.py:87
  247.9 6.2 fusion.167
  254.0 2.2 copy.256
  256.3 32.8 %while.81 = (s32[]{:T(128)}, f32[2,6,2048]{2,1,0:T(8,128)S(1)}, f32[3,1024]{1,0:T(4,128)S(1)}, f32[2,6,2048]{2,1,0:T(8,128)S(1)}, f32[3,1024]{1,0:T(4,128)S(1)},...) while((s32[]{:T(128)}, f32[2,6,2048]{2,1,0:T(8,128)S(1)}, ...), condition=%wide.region_17.18_spmd, body=%wide.region_10.17_spmd.sunk | while | flops 85970952 | bytes 499925 | solution.py:37
  256.4 16.2 fusion.187
  272.8 16.2 fusion.187
  290.1 2.3 convert_reduce_fusion
  292.5 2.2 copy.255
  294.7 32.8 %while.80 = (s32[]{:T(128)}, f32[2,6,2048]{2,1,0:T(8,128)S(1)}, f32[3,1024]{1,0:T(4,128)S(1)}, f32[2,6,2048]{2,1,0:T(8,128)S(1)}, f32[3,1024]{1,0:T(4,128)S(1)},...) while((s32[]{:T(128)}, f32[2,6,2048]{2,1,0:T(8,128)S(1)}, ...), condition=%wide.region_9.10_spmd, body=%wide.region_2.9_spmd.sunk | while | flops 85970952 | bytes 499925 | solution.py:37
  294.8 16.2 fusion.185
  311.2 16.2 fusion.185
  327.5 2.3 copy.257
  329.8 32.8 %while.82 = (s32[]{:T(128)}, f32[2,6,2048]{2,1,0:T(8,128)S(1)}, f32[3,1024]{1,0:T(4,128)S(1)}, f32[2,6,2048]{2,1,0:T(8,128)S(1)}, f32[3,1024]{1,0:T(4,128)S(1)},...) while((s32[]{:T(128)}, f32[2,6,2048]{2,1,0:T(8,128)S(1)}, ...), condition=%wide.region_26.27_spmd, body=%wide.region_19.26_spmd.sunk | while | flops 85970952 | bytes 499925 | solution.py:37
  329.9 16.2 fusion.189
  346.4 16.2 fusion.189
  363.3 32.9 %while.83 = (s32[]{:T(128)}, f32[2,6,2048]{2,1,0:T(8,128)S(1)}, f32[3,1024]{1,0:T(4,128)S(1)}, f32[2,6,2048]{2,1,0:T(8,128)S(1)}, f32[3,1024]{1,0:T(4,128)S(1)},...) while((s32[]{:T(128)}, f32[2,6,2048]{2,1,0:T(8,128)S(1)}, ...), condition=%wide.region_35.36_spmd, body=%wide.region_28.35_spmd.sunk | while | flops 85970952 | bytes 499925 | solution.py:37
  363.4 16.2 fusion.191
  379.9 16.2 fusion.191
  396.2 1.4 gather_fusion.1
  397.6 1.9 scatter_fusion.1
  399.8 97.2 %gather_fusion.15 = s32[16384]{0:T(1024)S(1)} fusion(s32[128]{0:T(128)S(1)} %get-tuple-element.733, s32[16384]{0:T(1024)S(1)} %broadcast_clamp_fusion.2), kind=kCustom, calls=%fused_computation.15 | custom fusion | bytes 196608 | tf_op jit(solution)/shard_map/gather | solution.py:84
  497.1 1.4 gather_fusion.10
  509.3 137.8 %all-reduce.11.cloned.1.call-done = f32[6,4096]{1,0:T(8,128)} async-done(((f32[6,4096]{1,0:T(8,128)}), f32[6,4096]{1,0:T(8,128)}) %all-reduce.11.cloned.1.call-update) | async-done | bytes 98320 | tf_op jit(solution)/shard_map/psum | solution.py:96
  647.2 0.9 constant_dynamic-update-slice_fusion.3
  648.1 141.3 %all-reduce.13.cloned.1.call-done = f32[6,4096]{1,0:T(8,128)} async-done(((f32[6,4096]{1,0:T(8,128)}), f32[6,4096]{1,0:T(8,128)}) %all-reduce.13.cloned.1.call-update) | async-done | bytes 98320 | tf_op jit(solution)/shard_map/psum | solution.py:96
  789.5 0.9 constant_dynamic-update-slice_fusion.2
  790.4 141.8 %all-reduce.15.cloned.1.call-done = f32[6,4096]{1,0:T(8,128)} async-done(((f32[6,4096]{1,0:T(8,128)}), f32[6,4096]{1,0:T(8,128)}) %all-reduce.15.cloned.1.call-update) | async-done | bytes 98320 | tf_op jit(solution)/shard_map/psum | solution.py:96
  933.4 1.4 scatter_fusion
  934.9 1.4 scatter_fusion.3
  936.4 1.4 scatter_fusion.2
  937.9 1.4 scatter_fusion.4
  941.9 59.0 %all-gather.3 = f32[128,6,256]{2,1,0:T(8,128)S(1)} all-gather(f32[1,6,256]{2,1,0:T(8,128)S(1)} %maximum_bitcast_fusion.1), channel_id=3, replica_groups=mesh['grp'=8,'dev'=16] {'grp','dev'}, dimensions={0}, use_global_device_ids=true | all-gather | bytes 792576 | tf_op jit(solution)/shard_map/all_gather | solution.py:85
  1000.9 8.4 copy.274
  1009.3 60.2 %gather_fusion.16 = f32[16384,6]{1,0:T(8,128)} fusion(f32[6,32768]{0,1:T(8,128)} %bitcast.633, s32[16384]{0:T(1024)S(1)} %broadcast_clamp_fusion), kind=kCustom, calls=%fused_computation.16 | custom fusion | bytes 851968 | tf_op jit(solution)/shard_map/gather | solution.py:87
  1069.4 6.2 fusion.166
  1075.6 2.2 copy.276
  1077.9 32.8 %while.84 = (s32[]{:T(128)}, f32[2,6,2048]{2,1,0:T(8,128)S(1)}, f32[3,1024]{1,0:T(4,128)S(1)}, f32[2,6,2048]{2,1,0:T(8,128)S(1)}, f32[3,1024]{1,0:T(4,128)S(1)},...) while((s32[]{:T(128)}, f32[2,6,2048]{2,1,0:T(8,128)S(1)}, ...), condition=%wide.region_52.53_spmd, body=%wide.region_45.52_spmd.sunk | while | flops 85970952 | bytes 499925 | solution.py:37
  1078.0 16.2 fusion.193
  1094.4 16.2 fusion.193
  1110.7 2.3 copy.279
  1113.6 34.0 %while.85 = (s32[]{:T(128)}, f32[2,6,2048]{2,1,0:T(8,128)}, f32[3,1024]{1,0:T(4,128)S(1)}, f32[2,6,2048]{2,1,0:T(8,128)S(1)}, f32[3,1024]{1,0:T(4,128)S(1)}, /*i...) while((s32[]{:T(128)}, f32[2,6,2048]{2,1,0:T(8,128)}, f32[3,1024]{1,0:T(4,128)S(1)}, ...), condition=%wide.region_60.61_spmd, body=%wide.region_53.60_spmd.sunk | while | flops 85970952 | bytes 483541 | solution.py:37
  1113.7 16.2 fusion.195
  1130.7 16.2 fusion.195
  1147.9 2.2 copy.282
  1150.1 32.8 %while.86 = (s32[]{:T(128)}, f32[2,6,2048]{2,1,0:T(8,128)S(1)}, f32[3,1024]{1,0:T(4,128)S(1)}, f32[2,6,2048]{2,1,0:T(8,128)S(1)}, f32[3,1024]{1,0:T(4,128)S(1)},...) while((s32[]{:T(128)}, f32[2,6,2048]{2,1,0:T(8,128)S(1)}, ...), condition=%wide.region_69.70_spmd, body=%wide.region_62.69_spmd.sunk | while | flops 85970952 | bytes 499925 | solution.py:37
  1150.2 16.2 fusion.197
  1166.6 16.2 fusion.197
  1183.7 32.8 %while.87 = (s32[]{:T(128)}, f32[2,6,2048]{2,1,0:T(8,128)S(1)}, f32[3,1024]{1,0:T(4,128)S(1)}, f32[2,6,2048]{2,1,0:T(8,128)S(1)}, f32[3,1024]{1,0:T(4,128)S(1)},...) while((s32[]{:T(128)}, f32[2,6,2048]{2,1,0:T(8,128)S(1)}, ...), condition=%wide.region_78.79_spmd, body=%wide.region_71.78_spmd.sunk | while | flops 85970952 | bytes 499925 | solution.py:37
  1183.8 16.2 fusion.199
  1200.2 16.2 fusion.199
  1219.8 66.7 %all-reduce.17.cloned.1.call-done = f32[6,4096]{1,0:T(8,128)} async-done(((f32[6,4096]{1,0:T(8,128)}), f32[6,4096]{1,0:T(8,128)}) %all-reduce.17.cloned.1.call-update) | async-done | bytes 98320 | tf_op jit(solution)/shard_map/psum | solution.py:96
  1287.5 141.8 %all-reduce.19.cloned.1.call-done = f32[6,4096]{1,0:T(8,128)} async-done(((f32[6,4096]{1,0:T(8,128)}), f32[6,4096]{1,0:T(8,128)}) %all-reduce.19.cloned.1.call-update) | async-done | bytes 98320 | tf_op jit(solution)/shard_map/psum | solution.py:96
  1430.3 141.2 %all-reduce.21.cloned.1.call-done = f32[6,4096]{1,0:T(8,128)} async-done(((f32[6,4096]{1,0:T(8,128)}), f32[6,4096]{1,0:T(8,128)}) %all-reduce.21.cloned.1.call-update) | async-done | bytes 98320 | tf_op jit(solution)/shard_map/psum | solution.py:96
  1571.5 0.9 constant_dynamic-update-slice_fusion.7
  1572.5 142.0 %all-reduce.23.cloned.1.call-done = f32[6,4096]{1,0:T(8,128)} async-done(((f32[6,4096]{1,0:T(8,128)}), f32[6,4096]{1,0:T(8,128)}) %all-reduce.23.cloned.1.call-update) | async-done | bytes 98320 | tf_op jit(solution)/shard_map/psum | solution.py:96
  1715.6 1.4 scatter_fusion.5
  1717.9 1.4 scatter_fusion.6
  1720.2 1.4 scatter_fusion.7
  1722.6 1.4 scatter_fusion.8
  (218 shorter events, 34.7 us)
Async XLA Ops:
  7.2 501.2 %all-reduce.9.cloned.1.call-start = ((), (), s32[]{:S(2)}) async-start(), calls=%async_computation | async-start | bytes 262144 | tf_op jit(solution)/shard_map/psum | solution.py:96
  78.7 11.5 copy-start.18
  289.1 0.6 copy-start.5
  289.8 357.4 %all-reduce.11.cloned.1.call-start = ((), (), s32[]{:S(2)}) async-start(), calls=%async_computation.1 | async-start | bytes 262144 | tf_op jit(solution)/shard_map/psum | solution.py:96
  327.5 2.3 copy-start.6
  362.7 0.7 copy-start.7
  396.2 100.8 %copy-start.8 = (f32[2,6,2048]{2,1,0:T(8,128)}, f32[2,6,2048]{2,1,0:T(8,128)S(1)}, u32[]{:S(2)}) copy-start(f32[2,6,2048]{2,1,0:T(8,128)S(1)} %get-tuple-element.238) | copy-start | bytes 294916
  397.6 543.1 %copy-start.15 = (s32[1024]{0:T(1024)}, s32[1024]{0:T(1024)S(1)}, u32[]{:S(2)}) copy-start(s32[1024]{0:T(1024)S(1)} %pad_clamp_fusion) | copy-start | bytes 12292
  399.7 99.4 %copy-start.11 = (f32[3,1024]{1,0:T(4,128)S(1)}, f32[3,1024]{1,0:T(4,128)}, u32[]{:S(2)}) copy-start(f32[3,1024]{1,0:T(4,128)} %param.23) | copy-start | bytes 36868
  399.7 99.6 %copy-start.12 = (f32[3,1024]{1,0:T(4,128)S(1)}, f32[3,1024]{1,0:T(4,128)}, u32[]{:S(2)}) copy-start(f32[3,1024]{1,0:T(4,128)} %param.25) | copy-start | bytes 36868
  399.7 99.8 %copy-start.13 = (f32[3,1024]{1,0:T(4,128)S(1)}, f32[3,1024]{1,0:T(4,128)}, u32[]{:S(2)}) copy-start(f32[3,1024]{1,0:T(4,128)} %param.24) | copy-start | bytes 36868
  399.7 100.7 %copy-start.14 = (f32[3,1024]{1,0:T(4,128)S(1)}, f32[3,1024]{1,0:T(4,128)}, u32[]{:S(2)}) copy-start(f32[3,1024]{1,0:T(4,128)} %param.26) | copy-start | bytes 36868
  508.4 281.0 %all-reduce.13.cloned.1.call-start = ((), (), s32[]{:S(2)}) async-start(), calls=%async_computation.2 | async-start | bytes 262144 | tf_op jit(solution)/shard_map/psum | solution.py:96
  647.2 285.0 %all-reduce.15.cloned.1.call-start = ((), (), s32[]{:S(2)}) async-start(), calls=%async_computation.3 | async-start | bytes 262144 | tf_op jit(solution)/shard_map/psum | solution.py:96
  789.4 497.1 %all-reduce.17.cloned.1.call-start = ((), (), s32[]{:S(2)}) async-start(), calls=%async_computation.4 | async-start | bytes 262144 | tf_op jit(solution)/shard_map/psum | solution.py:96
  934.7 74.5 %copy-start.2 = (f32[3,1024]{0,1:T(8,128)}, f32[3,1024]{0,1:T(8,128)S(1)}, u32[]{:S(2)}) copy-start(f32[3,1024]{0,1:T(8,128)S(1)} %scatter_fusion) | copy-start | bytes 36868
  936.3 73.0 %copy-start = (f32[3,1024]{0,1:T(8,128)}, f32[3,1024]{0,1:T(8,128)S(1)}, u32[]{:S(2)}) copy-start(f32[3,1024]{0,1:T(8,128)S(1)} %scatter_fusion.3) | copy-start | bytes 36868
  1110.7 2.9 copy-start.9
  1147.6 281.7 %all-reduce.19.cloned.1.call-start = ((), (), s32[]{:S(2)}) async-start(), calls=%async_computation.5 | async-start | bytes 262144 | tf_op jit(solution)/shard_map/psum | solution.py:96
  1183.0 0.7 copy-start.10
  1183.6 32.9 %copy-start.1 = (f32[3,1024]{0,1:T(8,128)S(1)}, f32[3,1024]{0,1:T(8,128)}, u32[]{:S(2)}) copy-start(f32[3,1024]{0,1:T(8,128)} %copy-done) | copy-start | bytes 36868
  1183.6 32.9 %copy-start.16 = (s32[1024]{0:T(1024)S(1)}, s32[1024]{0:T(1024)}, u32[]{:S(2)}) copy-start(s32[1024]{0:T(1024)} %copy-done.15) | copy-start | bytes 12292
  1183.6 34.3 %copy-start.3 = (f32[3,1024]{0,1:T(8,128)S(1)}, f32[3,1024]{0,1:T(8,128)}, u32[]{:S(2)}) copy-start(f32[3,1024]{0,1:T(8,128)} %copy-done.2) | copy-start | bytes 36868
  1183.6 531.7 %copy-start.19 = (f32[256]{0:T(256)S(1)}, f32[256]{0:T(256)}, u32[]{:S(2)}) copy-start(f32[256]{0:T(256)} %get-tuple-element.731) | copy-start | bytes 3076
  1183.6 531.7 %copy-start.20 = (f32[256]{0:T(256)S(1)}, f32[256]{0:T(256)}, u32[]{:S(2)}) copy-start(f32[256]{0:T(256)} %get-tuple-element.732) | copy-start | bytes 3076
  1183.7 531.9 %copy-start.17 = (s32[256,1]{0,1:T(1,128)S(1)}, s32[256,1]{0,1:T(1,128)}, u32[]{:S(2)}) copy-start(s32[256,1]{0,1:T(1,128)} %get-tuple-element.729) | copy-start | bytes 3076
  1216.5 355.0 %copy-start.4 = (f32[2,6,2048]{2,1,0:T(8,128)}, f32[2,6,2048]{2,1,0:T(8,128)S(1)}, u32[]{:S(2)}) copy-start(f32[2,6,2048]{2,1,0:T(8,128)S(1)} %get-tuple-element.248) | copy-start | bytes 294916
  1286.5 285.0 %all-reduce.21.cloned.1.call-start = ((), (), s32[]{:S(2)}) async-start(), calls=%async_computation.6 | async-start | bytes 262144 | tf_op jit(solution)/shard_map/psum | solution.py:96
  1429.3 285.1 %all-reduce.23.cloned.1.call-start = ((), (), s32[]{:S(2)}) async-start(), calls=%async_computation.7 | async-start | bytes 262144 | tf_op jit(solution)/shard_map/psum | solution.py:96
Sparse Core Ops, SparseCore 0:
  289.9 138.5 all-reduce.8
  508.5 138.5 all-reduce.10
  651.9 137.4 all-reduce.12
  794.7 137.4 all-reduce.14
  1147.8 138.6 all-reduce.16
  1291.8 137.4 all-reduce.18
  1434.0 137.4 all-reduce.20
  1577.0 137.4 all-reduce.22
where the time goes:
time: 1740 us; the launch traced here: 1730 us
  waiting for transfers between devices  913 us (52%)
  local copies, waits for them, and re-layouts  405 us (23%)
  other arithmetic  270 us (16%)
  blocking collectives  123 us (7%)
  between operations  19 us (1%)
    psum x8, waiting for transfers between devices, shards(): summed = lax.psum(terms, ('grp', 'dev'))  913 us
    reduce_sum x16, other arithmetic, pair_block(): jnp.sum(weight * (drift_z - along * gap_z), axis=1)  259 us
    gather x2, local copies, waits for them, and re-layouts, shards(): slot = owner * slot_cap + place - first[owner]  194 us
    all_gather x2, blocking collectives, shards(): gathered = lax.all_gather(targets[None], ('grp', 'dev'), axis=0, tiled=True)  123 us
    gather x2, local copies, waits for them, and re-layouts, shards(): compact = flat[:, slot]  120 us
  transfers between devices with their start and end apart: 8, of which 7 were waited for; matrix products, arithmetic and copies ran while one was open for 17% of the time, Pallas kernels for 0%

commit v1 on v0

--- a/solution.py
+++ b/solution.py
@@ -93,7 +93,8 @@
             if summed is not None:
                 terms, summed = lax.optimization_barrier((terms, summed))
                 parts.append(summed)
-            summed = lax.psum(terms, ("grp", "dev"))
+            inner = lax.psum(terms, "dev")
+            summed = lax.psum(inner, "grp")
         parts.append(summed)
         parts.append(jnp.zeros((6, slot_cap), jnp.float32))
         totals = jnp.concatenate(parts, axis=1)

time: 1740 us -> 1770 us (1.017)
  waiting for transfers between devices: 913 us -> 936 us
    psum x8 -> x16, waiting for transfers between devices: 913 us -> 936 us  [the longest x8 539 us: shards(): inner = lax.psum(terms, 'dev')]
  transfers between devices with their start and end apart: 8 -> 16, of which waited for: 7 -> 15; matrix products, arithmetic and copies ran while one was open for 17% -> 19% of each run, Pallas kernels for 0% -> 0%
where the time goes in v1:
time: 1770 us
  waiting for transfers between devices  936 us (53%)
  local copies, waits for them, and re-layouts  408 us (23%)
  other arithmetic  274 us (15%)
  blocking collectives  126 us (7%)
  between operations  18.9 us (1%)
    psum x8, waiting for transfers between devices, shards(): inner = lax.psum(terms, 'dev')  539 us
    psum x8, waiting for transfers between devices, shards(): summed = lax.psum(inner, 'grp')  397 us
    reduce_sum x16, other arithmetic, pair_block(): jnp.sum(weight * (drift_z - along * gap_z), axis=1)  262 us
    gather x2, local copies, waits for them, and re-layouts, shards(): slot = owner * slot_cap + place - first[owner]  194 us
    all_gather x2, blocking collectives, shards(): gathered = lax.all_gather(targets[None], ('grp', 'dev'), axis=0, tiled=True)  126 us
    gather x2, local copies, waits for them, and re-layouts, shards(): compact = flat[:, slot]  120 us
  transfers between devices with their start and end apart: 16, of which 15 were waited for; matrix products, arithmetic and copies ran while one was open for 19% of the time, Pallas kernels for 0%

profile of v1, /device:TPU:1, one launch (start us, length us, event | category | flops | bytes accessed | tf_op | source)
XLA Modules:
  0.0 1766.1 jit_solution(5579851974811496018)
XLA Ops:
  8.6 2.6 compare_select_fusion.4
  14.8 63.9 %all-gather.2 = f32[128,6,256]{2,1,0:T(8,128)S(1)} all-gather(f32[1,6,256]{2,1,0:T(8,128)S(1)} %maximum_bitcast_fusion), channel_id=2, replica_groups=mesh['grp'=8,'dev'=16] {'grp','dev'}, dimensions={0}, use_global_device_ids=true | all-gather | bytes 792576 | tf_op jit(solution)/shard_map/all_gather | solution.py:85
  78.7 8.4 copy.253
  87.8 2.3 convert_reduce_fusion.1
  90.3 97.2 %gather_fusion.6 = s32[16384]{0:T(1024)S(1)} fusion(s32[128]{0:T(128)S(1)} %get-tuple-element.734, s32[16384]{0:T(1024)S(1)} %broadcast_clamp_fusion.3), kind=kCustom, calls=%fused_computation.6 | custom fusion | bytes 196608 | tf_op jit(solution)/shard_map/gather | solution.py:84
  187.7 60.2 %gather_fusion.7 = f32[16384,6]{1,0:T(8,128)} fusion(f32[6,32768]{0,1:T(8,128)} %bitcast.632, s32[16384]{0:T(1024)S(1)} %broadcast_clamp_fusion.1), kind=kCustom, calls=%fused_computation.7 | custom fusion | bytes 851968 | tf_op jit(solution)/shard_map/gather | solution.py:87
  247.9 6.2 fusion.167
  254.0 2.2 copy.256
  256.3 32.9 %while.81 = (s32[]{:T(128)}, f32[2,6,2048]{2,1,0:T(8,128)S(1)}, f32[3,1024]{1,0:T(4,128)S(1)}, f32[2,6,2048]{2,1,0:T(8,128)S(1)}, f32[3,1024]{1,0:T(4,128)S(1)},...) while((s32[]{:T(128)}, f32[2,6,2048]{2,1,0:T(8,128)S(1)}, ...), condition=%wide.region_17.18_spmd, body=%wide.region_10.17_spmd.sunk | while | flops 85970952 | bytes 499925 | solution.py:37
  256.4 16.2 fusion.187
  272.8 16.2 fusion.187
  290.3 2.3 convert_reduce_fusion
  292.6 2.2 copy.255
  294.9 32.9 %while.80 = (s32[]{:T(128)}, f32[2,6,2048]{2,1,0:T(8,128)S(1)}, f32[3,1024]{1,0:T(4,128)S(1)}, f32[2,6,2048]{2,1,0:T(8,128)S(1)}, f32[3,1024]{1,0:T(4,128)S(1)},...) while((s32[]{:T(128)}, f32[2,6,2048]{2,1,0:T(8,128)S(1)}, ...), condition=%wide.region_9.10_spmd, body=%wide.region_2.9_spmd.sunk | while | flops 85970952 | bytes 499925 | solution.py:37
  295.0 16.2 fusion.185
  311.4 16.2 fusion.185
  327.8 2.3 copy.257
  330.1 32.8 %while.82 = (s32[]{:T(128)}, f32[2,6,2048]{2,1,0:T(8,128)S(1)}, f32[3,1024]{1,0:T(4,128)S(1)}, f32[2,6,2048]{2,1,0:T(8,128)S(1)}, f32[3,1024]{1,0:T(4,128)S(1)},...) while((s32[]{:T(128)}, f32[2,6,2048]{2,1,0:T(8,128)S(1)}, ...), condition=%wide.region_27.28_spmd, body=%wide.region_20.27_spmd.sunk | while | flops 85970952 | bytes 499925 | solution.py:37
  330.2 16.2 fusion.189
  346.6 16.2 fusion.189
  363.6 32.8 %while.83 = (s32[]{:T(128)}, f32[2,6,2048]{2,1,0:T(8,128)S(1)}, f32[3,1024]{1,0:T(4,128)S(1)}, f32[2,6,2048]{2,1,0:T(8,128)S(1)}, f32[3,1024]{1,0:T(4,128)S(1)},...) while((s32[]{:T(128)}, f32[2,6,2048]{2,1,0:T(8,128)S(1)}, ...), condition=%wide.region_37.38_spmd, body=%wide.region_30.37_spmd.sunk | while | flops 85970952 | bytes 499925 | solution.py:37
  363.7 16.2 fusion.191
  380.1 16.2 fusion.191
  396.6 97.2 %gather_fusion.15 = s32[16384]{0:T(1024)S(1)} fusion(s32[128]{0:T(128)S(1)} %get-tuple-element.733, s32[16384]{0:T(1024)S(1)} %broadcast_clamp_fusion.2), kind=kCustom, calls=%fused_computation.15 | custom fusion | bytes 196608 | tf_op jit(solution)/shard_map/gather | solution.py:84
  495.5 1.4 scatter_fusion.1
  496.9 53.2 %all-reduce.19.cloned.1.call-done = f32[6,4096]{1,0:T(8,128)} async-done(((f32[6,4096]{1,0:T(8,128)}), f32[6,4096]{1,0:T(8,128)}) %all-reduce.19.cloned.1.call-update) | async-done | bytes 98320 | tf_op jit(solution)/shard_map/psum | solution.py:97
  550.1 84.6 %all-reduce.21.cloned.1.call-done = f32[6,4096]{1,0:T(8,128)} async-done(((f32[6,4096]{1,0:T(8,128)}), f32[6,4096]{1,0:T(8,128)}) %all-reduce.21.cloned.1.call-update) | async-done | bytes 98320 | tf_op jit(solution)/shard_map/psum | solution.py:96
  641.8 53.6 %all-reduce.23.cloned.1.call-done = f32[6,4096]{1,0:T(8,128)} async-done(((f32[6,4096]{1,0:T(8,128)}), f32[6,4096]{1,0:T(8,128)}) %all-reduce.23.cloned.1.call-update) | async-done | bytes 98320 | tf_op jit(solution)/shard_map/psum | solution.py:97
  695.4 84.4 %all-reduce.25.cloned.1.call-done = f32[6,4096]{1,0:T(8,128)} async-done(((f32[6,4096]{1,0:T(8,128)}), f32[6,4096]{1,0:T(8,128)}) %all-reduce.25.cloned.1.call-update) | async-done | bytes 98320 | tf_op jit(solution)/shard_map/psum | solution.py:96
  780.9 59.6 %all-reduce.27.cloned.1.call-done = f32[6,4096]{1,0:T(8,128)} async-done(((f32[6,4096]{1,0:T(8,128)}), f32[6,4096]{1,0:T(8,128)}) %all-reduce.27.cloned.1.call-update) | async-done | bytes 98320 | tf_op jit(solution)/shard_map/psum | solution.py:97
  841.5 83.7 %all-reduce.29.cloned.1.call-done = f32[6,4096]{1,0:T(8,128)} async-done(((f32[6,4096]{1,0:T(8,128)}), f32[6,4096]{1,0:T(8,128)}) %all-reduce.29.cloned.1.call-update) | async-done | bytes 98320 | tf_op jit(solution)/shard_map/psum | solution.py:96
  926.1 59.8 %all-reduce.31.cloned.1.call-done = f32[6,4096]{1,0:T(8,128)} async-done(((f32[6,4096]{1,0:T(8,128)}), f32[6,4096]{1,0:T(8,128)}) %all-reduce.31.cloned.1.call-update) | async-done | bytes 98320 | tf_op jit(solution)/shard_map/psum | solution.py:97
  987.1 1.4 scatter_fusion
  988.6 1.4 scatter_fusion.3
  995.6 62.4 %all-gather.3 = f32[128,6,256]{2,1,0:T(8,128)S(1)} all-gather(f32[1,6,256]{2,1,0:T(8,128)S(1)} %maximum_bitcast_fusion.1), channel_id=3, replica_groups=mesh['grp'=8,'dev'=16] {'grp','dev'}, dimensions={0}, use_global_device_ids=true | all-gather | bytes 792576 | tf_op jit(solution)/shard_map/all_gather | solution.py:85
  1058.0 8.4 copy.274
  1066.4 60.2 %gather_fusion.16 = f32[16384,6]{1,0:T(8,128)} fusion(f32[6,32768]{0,1:T(8,128)} %bitcast.633, s32[16384]{0:T(1024)S(1)} %broadcast_clamp_fusion), kind=kCustom, calls=%fused_computation.16 | custom fusion | bytes 851968 | tf_op jit(solution)/shard_map/gather | solution.py:87
  1126.5 6.2 fusion.166
  1132.7 2.2 copy.279
  1135.0 35.4 %while.85 = (s32[]{:T(128)}, f32[2,6,2048]{2,1,0:T(8,128)S(1)}, f32[3,1024]{1,0:T(4,128)S(1)}, f32[2,6,2048]{2,1,0:T(8,128)S(1)}, f32[3,1024]{1,0:T(4,128)S(1)},...) while((s32[]{:T(128)}, f32[2,6,2048]{2,1,0:T(8,128)S(1)}, ...), condition=%wide.region_64.65_spmd, body=%wide.region_57.64_spmd.sunk | while | flops 85970952 | bytes 499925 | solution.py:37
  1135.1 16.8 fusion.195
  1152.8 16.8 fusion.195
  1171.1 2.1 gather_fusion.10
  1173.1 2.2 copy.276
  1175.4 75.3 %all-reduce.33.cloned.1.call-done = f32[6,4096]{1,0:T(8,128)} async-done(((f32[6,4096]{1,0:T(8,128)}), f32[6,4096]{1,0:T(8,128)}) %all-reduce.33.cloned.1.call-update) | async-done | bytes 98320 | tf_op jit(solution)/shard_map/psum | solution.py:96
  1251.0 35.4 %while.84 = (s32[]{:T(128)}, f32[2,6,2048]{2,1,0:T(8,128)S(1)}, f32[3,1024]{1,0:T(4,128)S(1)}, f32[2,6,2048]{2,1,0:T(8,128)S(1)}, f32[3,1024]{1,0:T(4,128)S(1)},...) while((s32[]{:T(128)}, f32[2,6,2048]{2,1,0:T(8,128)S(1)}, ...), condition=%wide.region_56.57_spmd, body=%wide.region_49.56_spmd.sunk | while | flops 85970952 | bytes 499925 | solution.py:37
  1251.1 16.8 fusion.193
  1268.8 16.8 fusion.193
  1286.4 24.9 %all-reduce.35.cloned.1.call-done = f32[6,4096]{1,0:T(8,128)} async-done(((f32[6,4096]{1,0:T(8,128)}), f32[6,4096]{1,0:T(8,128)}) %all-reduce.35.cloned.1.call-update) | async-done | bytes 98320 | tf_op jit(solution)/shard_map/psum | solution.py:97
  1315.1 2.2 copy.282
  1317.3 78.6 %all-reduce.37.cloned.1.call-done = f32[6,4096]{1,0:T(8,128)} async-done(((f32[6,4096]{1,0:T(8,128)}), f32[6,4096]{1,0:T(8,128)}) %all-reduce.37.cloned.1.call-update) | async-done | bytes 98320 | tf_op jit(solution)/shard_map/psum | solution.py:96
  1396.0 32.9 %while.86 = (s32[]{:T(128)}, f32[2,6,2048]{2,1,0:T(8,128)S(1)}, f32[3,1024]{1,0:T(4,128)S(1)}, f32[2,6,2048]{2,1,0:T(8,128)S(1)}, f32[3,1024]{1,0:T(4,128)S(1)},...) while((s32[]{:T(128)}, f32[2,6,2048]{2,1,0:T(8,128)S(1)}, ...), condition=%wide.region_74.75_spmd, body=%wide.region_67.74_spmd.sunk | while | flops 85970952 | bytes 499925 | solution.py:37
  1396.1 16.2 fusion.197
  1412.6 16.2 fusion.197
  1429.5 27.0 %all-reduce.39.cloned.1.call-done = f32[6,4096]{1,0:T(8,128)} async-done(((f32[6,4096]{1,0:T(8,128)}), f32[6,4096]{1,0:T(8,128)}) %all-reduce.39.cloned.1.call-update) | async-done | bytes 98320 | tf_op jit(solution)/shard_map/psum | solution.py:97
  1456.7 32.9 %while.87 = (s32[]{:T(128)}, f32[2,6,2048]{2,1,0:T(8,128)S(1)}, f32[3,1024]{1,0:T(4,128)S(1)}, f32[2,6,2048]{2,1,0:T(8,128)S(1)}, f32[3,1024]{1,0:T(4,128)S(1)},...) while((s32[]{:T(128)}, f32[2,6,2048]{2,1,0:T(8,128)S(1)}, ...), condition=%wide.region_84.85_spmd, body=%wide.region_77.84_spmd.sunk | while | flops 85970952 | bytes 499925 | solution.py:37
  1456.9 16.2 fusion.199
  1473.3 16.2 fusion.199
  1492.9 48.3 %all-reduce.41.cloned.1.call-done = f32[6,4096]{1,0:T(8,128)} async-done(((f32[6,4096]{1,0:T(8,128)}), f32[6,4096]{1,0:T(8,128)}) %all-reduce.41.cloned.1.call-update) | async-done | bytes 98320 | tf_op jit(solution)/shard_map/psum | solution.py:96
  1542.0 59.9 %all-reduce.43.cloned.1.call-done = f32[6,4096]{1,0:T(8,128)} async-done(((f32[6,4096]{1,0:T(8,128)}), f32[6,4096]{1,0:T(8,128)}) %all-reduce.43.cloned.1.call-update) | async-done | bytes 98320 | tf_op jit(solution)/shard_map/psum | solution.py:97
  1602.6 83.8 %all-reduce.45.cloned.1.call-done = f32[6,4096]{1,0:T(8,128)} async-done(((f32[6,4096]{1,0:T(8,128)}), f32[6,4096]{1,0:T(8,128)}) %all-reduce.45.cloned.1.call-update) | async-done | bytes 98320 | tf_op jit(solution)/shard_map/psum | solution.py:96
  1686.4 1.6 constant_dynamic-update-slice_fusion.7
  1688.0 59.0 %all-reduce.47.cloned.1.call-done = f32[6,4096]{1,0:T(8,128)} async-done(((f32[6,4096]{1,0:T(8,128)}), f32[6,4096]{1,0:T(8,128)}) %all-reduce.47.cloned.1.call-update) | async-done | bytes 98320 | tf_op jit(solution)/shard_map/psum | solution.py:97
  1747.0 1.6 constant_dynamic-update-slice_fusion.6
  (248 shorter events, 49.0 us)
Async XLA Ops:
  7.2 486.8 %all-reduce.17.cloned.1.call-start = ((), (), s32[]{:S(2)}) async-start(), calls=%async_computation | async-start | bytes 262144 | tf_op jit(solution)/shard_map/psum | solution.py:96
  78.7 11.5 copy-start.21
  289.1 0.6 copy-start.5
  289.8 260.3 %all-reduce.19.cloned.1.call-start = ((), (), s32[]{:S(2)}) async-start(), calls=%async_computation.1 | async-start | bytes 262144 | tf_op jit(solution)/shard_map/psum | solution.py:97
  327.7 2.3 copy-start.6
  362.9 0.7 copy-start.7
  396.4 97.4 %copy-start.8 = (f32[2,6,2048]{2,1,0:T(8,128)}, f32[2,6,2048]{2,1,0:T(8,128)S(1)}, u32[]{:S(2)}) copy-start(f32[2,6,2048]{2,1,0:T(8,128)S(1)} %get-tuple-element.238) | copy-start | bytes 294916
  396.6 238.4 %copy-start.14 = (f32[3,1024]{1,0:T(4,128)S(1)}, f32[3,1024]{1,0:T(4,128)}, u32[]{:S(2)}) copy-start(f32[3,1024]{1,0:T(4,128)} %param.23) | copy-start | bytes 36868
  396.6 238.7 %copy-start.15 = (f32[3,1024]{1,0:T(4,128)S(1)}, f32[3,1024]{1,0:T(4,128)}, u32[]{:S(2)}) copy-start(f32[3,1024]{1,0:T(4,128)} %param.25) | copy-start | bytes 36868
  396.6 238.9 %copy-start.16 = (f32[3,1024]{1,0:T(4,128)S(1)}, f32[3,1024]{1,0:T(4,128)}, u32[]{:S(2)}) copy-start(f32[3,1024]{1,0:T(4,128)} %param.24) | copy-start | bytes 36868
  396.6 239.7 %copy-start.17 = (f32[3,1024]{1,0:T(4,128)S(1)}, f32[3,1024]{1,0:T(4,128)}, u32[]{:S(2)}) copy-start(f32[3,1024]{1,0:T(4,128)} %param.26) | copy-start | bytes 36868
  494.0 140.7 %all-reduce.21.cloned.1.call-start = ((), (), s32[]{:S(2)}) async-start(), calls=%async_computation.2 | async-start | bytes 262144 | tf_op jit(solution)/shard_map/psum | solution.py:96
  550.1 145.3 %all-reduce.23.cloned.1.call-start = ((), (), s32[]{:S(2)}) async-start(), calls=%async_computation.3 | async-start | bytes 262144 | tf_op jit(solution)/shard_map/psum | solution.py:97
  634.8 145.1 %all-reduce.25.cloned.1.call-start = ((), (), s32[]{:S(2)}) async-start(), calls=%async_computation.4 | async-start | bytes 262144 | tf_op jit(solution)/shard_map/psum | solution.py:96
  695.4 145.1 %all-reduce.27.cloned.1.call-start = ((), (), s32[]{:S(2)}) async-start(), calls=%async_computation.5 | async-start | bytes 262144 | tf_op jit(solution)/shard_map/psum | solution.py:97
  695.4 370.9 %copy-start.18 = (s32[1024]{0:T(1024)}, s32[1024]{0:T(1024)S(1)}, u32[]{:S(2)}) copy-start(s32[1024]{0:T(1024)S(1)} %pad_clamp_fusion) | copy-start | bytes 12292
  779.9 145.3 %all-reduce.29.cloned.1.call-start = ((), (), s32[]{:S(2)}) async-start(), calls=%async_computation.6 | async-start | bytes 262144 | tf_op jit(solution)/shard_map/psum | solution.py:96
  840.5 145.4 %all-reduce.31.cloned.1.call-start = ((), (), s32[]{:S(2)}) async-start(), calls=%async_computation.7 | async-start | bytes 262144 | tf_op jit(solution)/shard_map/psum | solution.py:97
  925.2 325.5 %all-reduce.33.cloned.1.call-start = ((), (), s32[]{:S(2)}) async-start(), calls=%async_computation.8 | async-start | bytes 262144 | tf_op jit(solution)/shard_map/psum | solution.py:96
  988.4 77.9 %copy-start.2 = (f32[3,1024]{0,1:T(8,128)}, f32[3,1024]{0,1:T(8,128)S(1)}, u32[]{:S(2)}) copy-start(f32[3,1024]{0,1:T(8,128)S(1)} %scatter_fusion) | copy-start | bytes 36868
  990.0 76.4 %copy-start = (f32[3,1024]{0,1:T(8,128)}, f32[3,1024]{0,1:T(8,128)S(1)}, u32[]{:S(2)}) copy-start(f32[3,1024]{0,1:T(8,128)S(1)} %scatter_fusion.3) | copy-start | bytes 36868
  1170.4 0.6 copy-start.9
  1171.0 140.2 %all-reduce.35.cloned.1.call-start = ((), (), s32[]{:S(2)}) async-start(), calls=%async_computation.9 | async-start | bytes 262144 | tf_op jit(solution)/shard_map/psum | solution.py:97
  1250.7 145.3 %all-reduce.37.cloned.1.call-start = ((), (), s32[]{:S(2)}) async-start(), calls=%async_computation.10 | async-start | bytes 262144 | tf_op jit(solution)/shard_map/psum | solution.py:96
  1286.4 24.9 %copy-start.10 = (f32[2,6,2048]{2,1,0:T(8,128)}, f32[2,6,2048]{2,1,0:T(8,128)S(1)}, u32[]{:S(2)}) copy-start(f32[2,6,2048]{2,1,0:T(8,128)S(1)} %get-tuple-element.242) | copy-start | bytes 294916
  1311.3 145.3 %all-reduce.39.cloned.1.call-start = ((), (), s32[]{:S(2)}) async-start(), calls=%async_computation.11 | async-start | bytes 262144 | tf_op jit(solution)/shard_map/psum | solution.py:97
  1396.0 145.3 %all-reduce.41.cloned.1.call-start = ((), (), s32[]{:S(2)}) async-start(), calls=%async_computation.12 | async-start | bytes 262144 | tf_op jit(solution)/shard_map/psum | solution.py:96
  1428.9 27.7 %copy-start.11 = (f32[2,6,2048]{2,1,0:T(8,128)}, f32[2,6,2048]{2,1,0:T(8,128)S(1)}, u32[]{:S(2)}) copy-start(f32[2,6,2048]{2,1,0:T(8,128)S(1)} %get-tuple-element.245) | copy-start | bytes 294916
  1456.6 145.3 %all-reduce.43.cloned.1.call-start = ((), (), s32[]{:S(2)}) async-start(), calls=%async_computation.13 | async-start | bytes 262144 | tf_op jit(solution)/shard_map/psum | solution.py:97
  1456.7 33.0 %copy-start.1 = (f32[3,1024]{0,1:T(8,128)S(1)}, f32[3,1024]{0,1:T(8,128)}, u32[]{:S(2)}) copy-start(f32[3,1024]{0,1:T(8,128)} %copy-done) | copy-start | bytes 36868
  1456.7 33.0 %copy-start.19 = (s32[1024]{0:T(1024)S(1)}, s32[1024]{0:T(1024)}, u32[]{:S(2)}) copy-start(s32[1024]{0:T(1024)} %copy-done.18) | copy-start | bytes 12292
  1456.7 34.4 %copy-start.3 = (f32[3,1024]{0,1:T(8,128)S(1)}, f32[3,1024]{0,1:T(8,128)}, u32[]{:S(2)}) copy-start(f32[3,1024]{0,1:T(8,128)} %copy-done.2) | copy-start | bytes 36868
  1456.7 84.6 %copy-start.12 = (f32[6,4096]{1,0:T(8,128)S(1)}, f32[6,4096]{1,0:T(8,128)}, u32[]{:S(2)}) copy-start(f32[6,4096]{1,0:T(8,128)} %all-reduce.35.cloned.1.call-done) | copy-start | bytes 294916
  1456.7 145.2 %copy-start.13 = (f32[6,4096]{1,0:T(8,128)S(1)}, f32[6,4096]{1,0:T(8,128)}, u32[]{:S(2)}) copy-start(f32[6,4096]{1,0:T(8,128)} %all-reduce.39.cloned.1.call-done) | copy-start | bytes 294916
  1456.7 292.4 %copy-start.22 = (f32[256]{0:T(256)S(1)}, f32[256]{0:T(256)}, u32[]{:S(2)}) copy-start(f32[256]{0:T(256)} %get-tuple-element.731) | copy-start | bytes 3076
  1456.7 292.4 %copy-start.23 = (f32[256]{0:T(256)S(1)}, f32[256]{0:T(256)}, u32[]{:S(2)}) copy-start(f32[256]{0:T(256)} %get-tuple-element.732) | copy-start | bytes 3076
  1456.7 293.4 %copy-start.20 = (s32[256,1]{0,1:T(1,128)S(1)}, s32[256,1]{0,1:T(1,128)}, u32[]{:S(2)}) copy-start(s32[256,1]{0,1:T(1,128)} %get-tuple-element.729) | copy-start | bytes 3076
  1489.6 112.2 %copy-start.4 = (f32[2,6,2048]{2,1,0:T(8,128)}, f32[2,6,2048]{2,1,0:T(8,128)S(1)}, u32[]{:S(2)}) copy-start(f32[2,6,2048]{2,1,0:T(8,128)S(1)} %get-tuple-element.248) | copy-start | bytes 294916
  1541.3 145.1 %all-reduce.45.cloned.1.call-start = ((), (), s32[]{:S(2)}) async-start(), calls=%async_computation.14 | async-start | bytes 262144 | tf_op jit(solution)/shard_map/psum | solution.py:96
  1601.9 145.1 %all-reduce.47.cloned.1.call-start = ((), (), s32[]{:S(2)}) async-start(), calls=%async_computation.15 | async-start | bytes 262144 | tf_op jit(solution)/shard_map/psum | solution.py:97
Sparse Core Ops, SparseCore 0:
  289.9 79.0 all-reduce.16
  494.1 55.8 all-reduce.18
  553.3 81.4 all-reduce.20
  637.0 58.2 all-reduce.22
  698.4 81.4 all-reduce.24
  782.1 58.2 all-reduce.26
  843.7 81.4 all-reduce.28
  927.6 58.2 all-reduce.30
  1171.2 79.4 all-reduce.32
  1252.9 58.2 all-reduce.34
  1314.5 81.4 all-reduce.36
  1398.2 58.2 all-reduce.38
  1459.8 81.4 all-reduce.40
  1543.5 58.2 all-reduce.42
  1604.9 81.4 all-reduce.44
  1688.7 58.2 all-reduce.46
